TPU v7x, 128 devices: a whole 4x4x4 slice. The times are simulated.
128 devices in a mesh: chan: 32 (over y, z, x_lo), tm: 4 (over x_hi, core).
Axes of the slice: x: 4 (x_hi: 2, x_lo: 2; x = x_hi * 2 + x_lo), y: 4, z: 4, core: 2. Of those that a mesh axis runs over, the one named last changes fastest.
Arguments:
- record: float32 [64, 256, 16384], P('tm', 'chan'), may hold values from -6 to 6
- fir_taps: float32 [64], replicated, may hold values from -0.75 to 0.75
- pair_offsets: int32 [8], replicated, may hold values from -128 to 128, as said below
Outputs:
- correlation: float32 [8, 256, 16384], P('tm', None, 'chan')
Inputs may be any that keep to these rules, and one draw needn't show every extreme that they name: `pair_offsets`: 8 distinct nonzero channel offsets; both -128 and 128 are among them.
All inputs are finite; a program needn't handle non-finite values.
Results may differ from a plain program's by a relative error of at most 0.000098.
Values sent between devices are 32-bit elements; how exact they have to be, the bound alone decides.
No kernel may reach another device: no remote copies, remote signals or barrier semaphores. Data moves between devices by JAX's collectives and lax.ppermute only.
A program may use at most 192 MiB of HBM per device.

v0:
```python
import math

import jax
import jax.numpy as jnp
from jax import lax
from jax.experimental import pallas as pl
from jax.experimental.pallas import tpu as pltpu
from jax.sharding import PartitionSpec as P

S = 256
R = 128


PRECISE = lax.Precision.HIGHEST
FAST = lax.Precision.HIGH


def fir_matrix_of(fir_taps, seg_len):
    row_ids = lax.broadcasted_iota(jnp.int32, (seg_len, seg_len), 0)
    col_ids = lax.broadcasted_iota(jnp.int32, (seg_len, seg_len), 1)
    spread = col_ids - row_ids
    tap_ids = lax.broadcasted_iota(jnp.int32, (1, 1, fir_taps.shape[0]), 2)
    hits = spread[:, :, None] == tap_ids
    return jnp.sum(jnp.where(hits, fir_taps[None, None, :], 0.0), axis=2)


def forward_table(seg_len):
    length = 2 * seg_len
    time_ids = lax.broadcasted_iota(jnp.int32, (seg_len, length), 0)
    slot_ids = lax.broadcasted_iota(jnp.int32, (seg_len, length), 1)
    frequency = jnp.where(slot_ids <= seg_len, slot_ids, slot_ids - seg_len)
    angles = (frequency * time_ids % length).astype(jnp.float32) * (2.0 * math.pi / length)
    return jnp.where(slot_ids <= seg_len, jnp.cos(angles), jnp.sin(angles))


def inverse_table(seg_len, norm_scale):
    length = 2 * seg_len
    slot_ids = lax.broadcasted_iota(jnp.int32, (3 * seg_len, seg_len), 0)
    lag_ids = lax.broadcasted_iota(jnp.int32, (3 * seg_len, seg_len), 1) - seg_len // 2
    cosine_rows = slot_ids < length
    frequency = jnp.where(
        cosine_rows, jnp.where(slot_ids <= seg_len, slot_ids, slot_ids - seg_len), slot_ids - length
    )
    angles = (frequency * lag_ids % length).astype(jnp.float32) * (2.0 * math.pi / length)
    edge_rows = (slot_ids == 0) | (slot_ids == seg_len)
    cosine_weights = jnp.where(edge_rows, 1.0 / length, 2.0 / length)
    sine_weights = jnp.where(frequency == 0, 0.0, -2.0 / length)
    values = jnp.where(
        cosine_rows, cosine_weights * jnp.cos(angles), sine_weights * jnp.sin(angles)
    )
    return values * norm_scale


def halo(array, axis, dim, width):
    size, length = (lax.axis_size(axis), array.shape[dim])
    up = [(i, (i + 1) % size) for i in range(size)]
    down = [(j, i) for i, j in up]
    last = lax.slice_in_dim(array, length - width, length, axis=dim)
    first = lax.slice_in_dim(array, 0, width, axis=dim)
    before = lax.ppermute(last, axis, up)
    after = lax.ppermute(first, axis, down)
    return jnp.concatenate([before, array, after], axis=dim)


CHUNKS = 4


def cross_kernel(offs_ref, spec_ref, acc_ref, out_ref):
    segs, ext, width = spec_ref.shape
    half = width // 2
    start = R + offs_ref[pl.program_id(0)]
    rem = start % 8
    base = start - rem
    turn = (8 - rem) % 8
    keep = lax.broadcasted_iota(jnp.int32, (8, width), 0) < 8 - rem

    def body(r, carry):
        r0 = pl.multiple_of(R + r * 8, 8)
        p0 = pl.multiple_of(base + r * 8, 8)
        p1 = pl.multiple_of(jnp.minimum(p0 + 8, ext - 8), 8)
        o0 = pl.multiple_of(r * 8, 8)
        acc_m = acc_ref[pl.ds(o0, 8), 0:width]
        acc_lo = jnp.zeros((8, half), jnp.float32)
        acc_hi = acc_ref[pl.ds(o0, 8), width:]
        for s in range(segs):
            a = spec_ref[s, pl.ds(r0, 8), :]
            b0 = pltpu.roll(spec_ref[s, pl.ds(p0, 8), :], turn, 0)
            b1 = pltpu.roll(spec_ref[s, pl.ds(p1, 8), :], turn, 0)
            b = jnp.where(keep, b0, b1)
            acc_m = acc_m + a * b
            acc_lo = acc_lo + a[:, :half] * b[:, half:]
            acc_hi = acc_hi + a[:, half:] * b[:, :half]
        out_ref[pl.ds(o0, 8), 0:width] = acc_m
        out_ref[pl.ds(o0, 8), width:] = acc_hi - acc_lo
        return carry

    lax.fori_loop(0, (ext - 2 * R) // 8, body, 0, unroll=2)


def cross_spectra(spectra, offsets, acc):
    segs, ext, width = spectra.shape
    n_k, own_w, out_w = acc.shape
    grid_spec = pltpu.PrefetchScalarGridSpec(
        num_scalar_prefetch=1,
        grid=(n_k,),
        in_specs=[
            pl.BlockSpec(
                (segs, ext, width), lambda k, offs: (0, 0, 0), pipeline_mode=pl.Buffered(1)
            ),
            pl.BlockSpec((None, own_w, out_w), lambda k, offs: (k, 0, 0)),
        ],
        out_specs=pl.BlockSpec((None, own_w, out_w), lambda k, offs: (k, 0, 0)),
    )
    return pl.pallas_call(
        cross_kernel,
        grid_spec=grid_spec,
        out_shape=jax.ShapeDtypeStruct(acc.shape, jnp.float32),
        input_output_aliases={2: 0},
        compiler_params=pltpu.CompilerParams(
            dimension_semantics=("arbitrary",), vmem_limit_bytes=48 * 1024 * 1024
        ),
    )(offsets, spectra, acc)


def windows(piece, n_chan, width):
    segs, rows, channels = piece.shape
    blocks = piece.reshape(segs, rows, n_chan, channels // n_chan)
    before = jnp.roll(blocks, 1, axis=2)[..., -width:]
    after = jnp.roll(blocks, -1, axis=2)[..., :width]
    return jnp.concatenate([before, blocks, after], axis=3).transpose(2, 0, 1, 3)


def per_device(record, fir_taps, pair_offsets):
    n_chan = lax.axis_size("chan")
    n_time = lax.axis_size("tm")
    seg_count, part_rows, channels = record.shape
    block_width = channels // n_chan
    table = jnp.dot(fir_matrix_of(fir_taps, S), forward_table(S), precision=PRECISE)
    table = table.reshape(n_chan, part_rows, 2 * S)
    norm_scale = 1.0 / math.sqrt(seg_count * n_time * S)
    inverse = inverse_table(S, norm_scale)
    inverse_cat = jnp.concatenate([inverse[: 2 * S], inverse[2 * S :]], axis=0)
    even_offsets = pair_offsets[0::2]
    odd_offsets = pair_offsets[1::2]
    acc_shape = (even_offsets.shape[0], block_width, 3 * S)
    even = jnp.zeros(acc_shape, jnp.float32)
    odd = jnp.zeros(acc_shape, jnp.float32)
    step = seg_count // CHUNKS

    def exchange(g):
        piece = windows(lax.dynamic_slice_in_dim(record, g * step, step, 0), n_chan, R)
        return lax.all_to_all(piece, "chan", split_axis=0, concat_axis=0, tiled=True)

    def accumulate(turned, even, odd):
        spectra = jnp.einsum("asuc,auj->scj", turned, table, precision=FAST)
        return cross_spectra(spectra, even_offsets, even), cross_spectra(spectra, odd_offsets, odd)

    def body(g, carry):
        turned, even, odd = carry
        upcoming = exchange(g + 1)
        even, odd = accumulate(turned, even, odd)
        return upcoming, even, odd

    turned, even, odd = lax.fori_loop(0, CHUNKS - 1, body, (exchange(0), even, odd))
    even, odd = accumulate(turned, even, odd)

    def finish(crossed):
        lagged = jnp.einsum("kcr,rl->klc", crossed, inverse_cat, precision=FAST)
        return lax.psum_scatter(lagged, "tm", scatter_dimension=0, tiled=True)

    first = finish(even)
    second = finish(odd)
    return jnp.concatenate([first, second], axis=0)


def solution(mesh):
    placed = (P("tm", "chan", None), P(), P())
    return jax.shard_map(
        per_device, mesh=mesh, in_specs=placed, out_specs=P("tm", None, "chan"), check_vma=False
    )
```

profile of v0, /device:TPU:1, one launch (start us, length us, event | category | flops | bytes accessed | tf_op | source)
XLA Modules:
  0.0 368.9 jit_solution(1564378493181942298)
XLA Ops:
  6.5 1.6 slice-done
  8.1 1.2 copy.27
  10.3 3.5 copy.19
  13.8 10.0 %all-to-all-start.1 = ((f32[32,4,8,768]{3,2,1,0:T(8,128)}), f32[32,4,8,768]{3,2,1,0:T(8,128)}, u32[]{:S(2)}, u32[]{:S(2)}) async-start(f32[32,4,8,768]{3,2,1,0:T(8,128)} %copy.19), calls=%async_computation.1 | async-start | bytes 6291456 | tf_op jit(solution)/shard_map/all_to_all | solution.py:152
  24.7 0.6 iota_compare_fusion.1
  25.3 0.6 fusion.34
  25.9 0.6 iota_add_fusion
  26.5 5.7 %select_reduce_fusion = f32[256,256]{1,0:T(8,128)S(1)} fusion(f32[64]{0:T(128)S(1)} %copy-done.6, s32[256,256]{1,0:T(8,128)S(1)} %iota_subtract_fusion), kind=kLoop, calls=%fused_computation.9 | loop fusion | flops 12517376 | bytes 524544 | tf_op jit(solution)/shard_map/reduce_sum | solution.py:24
  32.3 3.8 %fusion.17 = f32[32,8,512]{2,1,0:T(8,128)} fusion(f32[256,256]{1,0:T(8,128)S(1)} %select_reduce_fusion, s32[512]{0:T(512)S(1)} %iota_add_fusion.2, pred[512]{0:T(512)(128)(4,1)S(1)} %iota_compare_fusion.5), kind=kOutput, calls=%fused_computation.39 | convolution fusion | flops 404750336 | bytes 788992 | tf_op jit(solution)/shard_map/dot_general | solution.py:138
  36.0 35.5 %all-to-all-done.1 = f32[32,4,8,768]{3,2,1,0:T(8,128)} async-done(((f32[32,4,8,768]{3,2,1,0:T(8,128)}), f32[32,4,8,768]{3,2,1,0:T(8,128)}, u32[]{:S(2)}, u32[]{:S(2)}) %all-to-all-start.1) | async-done | bytes 3145760 | tf_op jit(solution)/shard_map/all_to_all | solution.py:152
  71.5 3.2 broadcast.70
  74.7 3.1 broadcast.70.clone
  77.8 171.6 %while.17 = (s32[]{:T(128)}, f32[32,4,8,768]{3,2,1,0:T(8,128)}, f32[4,512,768]{2,1,0:T(8,128)}, f32[4,512,768]{2,1,0:T(8,128)}, f32[16,8,16384]{2,1,0:T(8,128)},...) while((s32[]{:T(128)}, f32[32,4,8,768]{3,2,1,0:T(8,128)}, ...), condition=%wide.region_2.3_spmd, body=%wide.region_1.2_spmd.sunk | while | flops 2419064832 | bytes 58196168 | solution.py:164
  77.8 1.7 constant_dynamic-slice_fusion.2
  79.6 1.2 copy.30
  81.8 3.5 copy.31
  85.3 4.1 %all-to-all-start = ((f32[32,4,8,768]{3,2,1,0:T(8,128)}), f32[32,4,8,768]{3,2,1,0:T(8,128)S(1)}, u32[]{:S(2)}, u32[]{:S(2)}) async-start(f32[32,4,8,768]{3,2,1,0:T(8,128)} %copy.31), calls=%async_computation | async-start | bytes 6291456 | tf_op jit(solution)/shard_map/while/body/eval_jaxpr/all_to_all | solution.py:152
  89.4 7.3 %convolution_bitcast_fusion.5.spec_ref = f32[4,768,512]{2,1,0:T(8,128)} fusion(f32[32,4,8,768]{3,2,1,0:T(8,128)} %get-tuple-element.253, f32[32,8,512]{2,1,0:T(8,128)} %get-tuple-element.269), kind=kOutput, calls=%fused_computation.5.clone.1 | convolution fusion | flops 2415919104 | bytes 9961472 | tf_op jit(solution)/shard_map/while/body/eval_jaxpr/asuc,auj->scj/dot_general | solution.py:155
  96.7 11.3 %eval_jaxpr.10 = f32[4,512,768]{2,1,0:T(8,128)} custom-call(s32[4]{0:T(128)S(1)} %get-tuple-element.270.offs_ref, f32[4,768,512]{2,1,0:T(8,128)} %convolution_bitcast_fusion.5.spec_ref, f32[4,512,768]{2,1,0:T(8,128)} %get-tuple-element.254.acc_ref), custom_call_target="tpu_custom_call", output_to_operand_aliasing={{}: (2, {})} | custom-call | tf_op jit(solution)/shard_map/while/body/eval_jaxpr/pallas_call | solution.py:114
  108.0 11.4 %eval_jaxpr.11 = f32[4,512,768]{2,1,0:T(8,128)} custom-call(s32[4]{0:T(128)S(1)} %get-tuple-element.271.offs_ref, f32[4,768,512]{2,1,0:T(8,128)} %convolution_bitcast_fusion.5.spec_ref, f32[4,512,768]{2,1,0:T(8,128)} %get-tuple-element.255.acc_ref), custom_call_target="tpu_custom_call", output_to_operand_aliasing={{}: (2, {})} | custom-call | tf_op jit(solution)/shard_map/while/body/eval_jaxpr/pallas_call | solution.py:114
  119.4 14.5 %all-to-all-done = f32[32,4,8,768]{3,2,1,0:T(8,128)S(1)} async-done(((f32[32,4,8,768]{3,2,1,0:T(8,128)}), f32[32,4,8,768]{3,2,1,0:T(8,128)S(1)}, u32[]{:S(2)}, u32[]{:S(2)}) %all-to-all-start) | async-done | bytes 3145760 | tf_op jit(solution)/shard_map/while/body/eval_jaxpr/all_to_all | solution.py:152
  133.8 1.7 copy.43
  135.5 1.7 constant_dynamic-slice_fusion.2
  137.2 1.2 copy.30
  139.5 3.5 copy.31
  143.0 4.1 %all-to-all-start = ((f32[32,4,8,768]{3,2,1,0:T(8,128)}), f32[32,4,8,768]{3,2,1,0:T(8,128)S(1)}, u32[]{:S(2)}, u32[]{:S(2)}) async-start(f32[32,4,8,768]{3,2,1,0:T(8,128)} %copy.31), calls=%async_computation | async-start | bytes 6291456 | tf_op jit(solution)/shard_map/while/body/eval_jaxpr/all_to_all | solution.py:152
  147.0 7.3 %convolution_bitcast_fusion.5.spec_ref = f32[4,768,512]{2,1,0:T(8,128)} fusion(f32[32,4,8,768]{3,2,1,0:T(8,128)} %get-tuple-element.253, f32[32,8,512]{2,1,0:T(8,128)} %get-tuple-element.269), kind=kOutput, calls=%fused_computation.5.clone.1 | convolution fusion | flops 2415919104 | bytes 9961472 | tf_op jit(solution)/shard_map/while/body/eval_jaxpr/asuc,auj->scj/dot_general | solution.py:155
  154.3 11.3 %eval_jaxpr.10 = f32[4,512,768]{2,1,0:T(8,128)} custom-call(s32[4]{0:T(128)S(1)} %get-tuple-element.270.offs_ref, f32[4,768,512]{2,1,0:T(8,128)} %convolution_bitcast_fusion.5.spec_ref, f32[4,512,768]{2,1,0:T(8,128)} %get-tuple-element.254.acc_ref), custom_call_target="tpu_custom_call", output_to_operand_aliasing={{}: (2, {})} | custom-call | tf_op jit(solution)/shard_map/while/body/eval_jaxpr/pallas_call | solution.py:114
  165.7 11.4 %eval_jaxpr.11 = f32[4,512,768]{2,1,0:T(8,128)} custom-call(s32[4]{0:T(128)S(1)} %get-tuple-element.271.offs_ref, f32[4,768,512]{2,1,0:T(8,128)} %convolution_bitcast_fusion.5.spec_ref, f32[4,512,768]{2,1,0:T(8,128)} %get-tuple-element.255.acc_ref), custom_call_target="tpu_custom_call", output_to_operand_aliasing={{}: (2, {})} | custom-call | tf_op jit(solution)/shard_map/while/body/eval_jaxpr/pallas_call | solution.py:114
  177.0 15.3 %all-to-all-done = f32[32,4,8,768]{3,2,1,0:T(8,128)S(1)} async-done(((f32[32,4,8,768]{3,2,1,0:T(8,128)}), f32[32,4,8,768]{3,2,1,0:T(8,128)S(1)}, u32[]{:S(2)}, u32[]{:S(2)}) %all-to-all-start) | async-done | bytes 3145760 | tf_op jit(solution)/shard_map/while/body/eval_jaxpr/all_to_all | solution.py:152
  192.4 1.7 copy.43
  194.1 1.7 constant_dynamic-slice_fusion.2
  195.8 1.2 copy.30
  198.0 3.5 copy.31
  201.5 4.1 %all-to-all-start = ((f32[32,4,8,768]{3,2,1,0:T(8,128)}), f32[32,4,8,768]{3,2,1,0:T(8,128)S(1)}, u32[]{:S(2)}, u32[]{:S(2)}) async-start(f32[32,4,8,768]{3,2,1,0:T(8,128)} %copy.31), calls=%async_computation | async-start | bytes 6291456 | tf_op jit(solution)/shard_map/while/body/eval_jaxpr/all_to_all | solution.py:152
  205.6 7.3 %convolution_bitcast_fusion.5.spec_ref = f32[4,768,512]{2,1,0:T(8,128)} fusion(f32[32,4,8,768]{3,2,1,0:T(8,128)} %get-tuple-element.253, f32[32,8,512]{2,1,0:T(8,128)} %get-tuple-element.269), kind=kOutput, calls=%fused_computation.5.clone.1 | convolution fusion | flops 2415919104 | bytes 9961472 | tf_op jit(solution)/shard_map/while/body/eval_jaxpr/asuc,auj->scj/dot_general | solution.py:155
  212.9 11.3 %eval_jaxpr.10 = f32[4,512,768]{2,1,0:T(8,128)} custom-call(s32[4]{0:T(128)S(1)} %get-tuple-element.270.offs_ref, f32[4,768,512]{2,1,0:T(8,128)} %convolution_bitcast_fusion.5.spec_ref, f32[4,512,768]{2,1,0:T(8,128)} %get-tuple-element.254.acc_ref), custom_call_target="tpu_custom_call", output_to_operand_aliasing={{}: (2, {})} | custom-call | tf_op jit(solution)/shard_map/while/body/eval_jaxpr/pallas_call | solution.py:114
  224.2 11.4 %eval_jaxpr.11 = f32[4,512,768]{2,1,0:T(8,128)} custom-call(s32[4]{0:T(128)S(1)} %get-tuple-element.271.offs_ref, f32[4,768,512]{2,1,0:T(8,128)} %convolution_bitcast_fusion.5.spec_ref, f32[4,512,768]{2,1,0:T(8,128)} %get-tuple-element.255.acc_ref), custom_call_target="tpu_custom_call", output_to_operand_aliasing={{}: (2, {})} | custom-call | tf_op jit(solution)/shard_map/while/body/eval_jaxpr/pallas_call | solution.py:114
  235.6 12.1 %all-to-all-done = f32[32,4,8,768]{3,2,1,0:T(8,128)S(1)} async-done(((f32[32,4,8,768]{3,2,1,0:T(8,128)}), f32[32,4,8,768]{3,2,1,0:T(8,128)S(1)}, u32[]{:S(2)}, u32[]{:S(2)}) %all-to-all-start) | async-done | bytes 3145760 | tf_op jit(solution)/shard_map/while/body/eval_jaxpr/all_to_all | solution.py:152
  247.7 1.7 copy.43
  249.4 7.3 %convolution_bitcast_fusion.1.spec_ref = f32[4,768,512]{2,1,0:T(8,128)} fusion(f32[32,4,8,768]{3,2,1,0:T(8,128)} %get-tuple-element.136, f32[32,8,512]{2,1,0:T(8,128)} %get-tuple-element.289), kind=kOutput, calls=%fused_computation.16 | convolution fusion | flops 2415919104 | bytes 9961472 | tf_op jit(solution)/shard_map/asuc,auj->scj/dot_general | solution.py:155
  256.8 11.3 %shard_map.37 = f32[4,512,768]{2,1,0:T(8,128)} custom-call(s32[4]{0:T(128)S(1)} %get-tuple-element.288, f32[4,768,512]{2,1,0:T(8,128)} %convolution_bitcast_fusion.1.spec_ref, f32[4,512,768]{2,1,0:T(8,128)} %get-tuple-element.137.acc_ref), custom_call_target="tpu_custom_call", output_to_operand_aliasing={{}: (2, {})} | custom-call | tf_op jit(solution)/shard_map/pallas_call | solution.py:114
  268.1 9.9 %convolution_bitcast_fusion.3 = f32[4,256,512]{2,1,0:T(8,128)} fusion(f32[4,512,768]{2,1,0:T(8,128)} %shard_map.37, s32[256]{0:T(256)S(1)} %copy-done.5, s32[768]{0:T(1024)S(1)} %copy-done.1, s32[768]{0:T(1024)S(1)} %copy-done.2, f32[768]{0:T(1024)S(1)} %copy-done, pred[768]{0:T(1024)(128)(4,1)S(1)} %copy-done.3, pred[768]{0:T(1024)(128)(4,1)S(1)} %copy-done.4), kind=kOutput, calls=%fused_computation.19 | convolution fusion | flops 2420244480 | bytes 8400384 | tf_op jit(solution)/shard_map/kcr,rl->klc/dot_general | solution.py:168
  278.2 11.6 %shard_map.38 = f32[4,512,768]{2,1,0:T(8,128)} custom-call(s32[4]{0:T(128)S(1)} %get-tuple-element.287, f32[4,768,512]{2,1,0:T(8,128)} %convolution_bitcast_fusion.1.spec_ref, f32[4,512,768]{2,1,0:T(8,128)} %get-tuple-element.138.acc_ref), custom_call_target="tpu_custom_call", output_to_operand_aliasing={{}: (2, {})} | custom-call | tf_op jit(solution)/shard_map/pallas_call | solution.py:114
  289.8 10.3 %convolution_bitcast_fusion.2 = f32[4,256,512]{2,1,0:T(8,128)} fusion(f32[4,512,768]{2,1,0:T(8,128)} %shard_map.38, s32[256]{0:T(256)S(1)} %copy-done.5, s32[768]{0:T(1024)S(1)} %copy-done.1, s32[768]{0:T(1024)S(1)} %copy-done.2, f32[768]{0:T(1024)S(1)} %copy-done, pred[768]{0:T(1024)(128)(4,1)S(1)} %copy-done.3, pred[768]{0:T(1024)(128)(4,1)S(1)} %copy-done.4), kind=kOutput, calls=%fused_computation.18 | convolution fusion | flops 2420244480 | bytes 8400384 | tf_op jit(solution)/shard_map/kcr,rl->klc/dot_general | solution.py:168
  300.1 19.6 %reduce-scatter.3.cloned.1.call-done = f32[1,256,512]{2,1,0:T(8,128)} async-done(((f32[4,256,512]{2,1,0:T(8,128)}), f32[1,256,512]{2,1,0:T(8,128)}) %reduce-scatter.3.cloned.1.call-update) | async-done | bytes 524304 | tf_op jit(solution)/shard_map/reduce_scatter | solution.py:169
  319.7 40.2 %reduce-scatter.5.cloned.1.call-done = f32[1,256,512]{2,1,0:T(8,128)} async-done(((f32[4,256,512]{2,1,0:T(8,128)}), f32[1,256,512]{2,1,0:T(8,128)}) %reduce-scatter.5.cloned.1.call-update) | async-done | bytes 524304 | tf_op jit(solution)/shard_map/reduce_scatter | solution.py:169
  359.8 2.2 pad_maximum_fusion.4
  (39 shorter events, 4.9 us)
Async XLA Ops:
  6.5 1.6 slice-start
  13.8 10.1 %copy-start.7 = (s32[8]{0:T(128)S(1)}, s32[8]{0:T(128)}, u32[]{:S(2)}) copy-start(s32[8]{0:T(128)} %param.7) | copy-start | bytes 100
  13.8 12.7 %copy-start.6 = (f32[64]{0:T(128)S(1)}, f32[64]{0:T(128)}, u32[]{:S(2)}) copy-start(f32[64]{0:T(128)} %param.6) | copy-start | bytes 772
  13.8 57.7 %all-to-all-start.1 = ((f32[32,4,8,768]{3,2,1,0:T(8,128)}), f32[32,4,8,768]{3,2,1,0:T(8,128)}, u32[]{:S(2)}, u32[]{:S(2)}) async-start(f32[32,4,8,768]{3,2,1,0:T(8,128)} %copy.19), calls=%async_computation.1 | async-start | bytes 6291456 | tf_op jit(solution)/shard_map/all_to_all | solution.py:152
  23.9 295.8 %reduce-scatter.3.cloned.1.call-start = ((), (), s32[]{:S(2)}) async-start(), calls=%async_computation.4 | async-start | bytes 2621440 | tf_op jit(solution)/shard_map/reduce_scatter | solution.py:169
  85.3 48.5 %all-to-all-start = ((f32[32,4,8,768]{3,2,1,0:T(8,128)}), f32[32,4,8,768]{3,2,1,0:T(8,128)S(1)}, u32[]{:S(2)}, u32[]{:S(2)}) async-start(f32[32,4,8,768]{3,2,1,0:T(8,128)} %copy.31), calls=%async_computation | async-start | bytes 6291456 | tf_op jit(solution)/shard_map/while/body/eval_jaxpr/all_to_all | solution.py:152
  143.0 49.4 %all-to-all-start = ((f32[32,4,8,768]{3,2,1,0:T(8,128)}), f32[32,4,8,768]{3,2,1,0:T(8,128)S(1)}, u32[]{:S(2)}, u32[]{:S(2)}) async-start(f32[32,4,8,768]{3,2,1,0:T(8,128)} %copy.31), calls=%async_computation | async-start | bytes 6291456 | tf_op jit(solution)/shard_map/while/body/eval_jaxpr/all_to_all | solution.py:152
  201.5 46.2 %all-to-all-start = ((f32[32,4,8,768]{3,2,1,0:T(8,128)}), f32[32,4,8,768]{3,2,1,0:T(8,128)S(1)}, u32[]{:S(2)}, u32[]{:S(2)}) async-start(f32[32,4,8,768]{3,2,1,0:T(8,128)} %copy.31), calls=%async_computation | async-start | bytes 6291456 | tf_op jit(solution)/shard_map/while/body/eval_jaxpr/all_to_all | solution.py:152
  256.7 11.4 %copy-start = (f32[768]{0:T(1024)S(1)}, f32[768]{0:T(1024)}, u32[]{:S(2)}) copy-start(f32[768]{0:T(1024)} %fusion.34) | copy-start | bytes 9220
  256.7 11.4 %copy-start.1 = (s32[768]{0:T(1024)S(1)}, s32[768]{0:T(1024)}, u32[]{:S(2)}) copy-start(s32[768]{0:T(1024)} %get-tuple-element.179) | copy-start | bytes 9220
  256.7 11.4 %copy-start.2 = (s32[768]{0:T(1024)S(1)}, s32[768]{0:T(1024)}, u32[]{:S(2)}) copy-start(s32[768]{0:T(1024)} %get-tuple-element.180) | copy-start | bytes 9220
  256.7 11.4 %copy-start.3 = (pred[768]{0:T(1024)(128)(4,1)S(1)}, pred[768]{0:T(1024)(128)(4,1)}, u32[]{:S(2)}) copy-start(pred[768]{0:T(1024)(128)(4,1)} %get-tuple-element.181) | copy-start | bytes 2308
  256.7 11.4 %copy-start.4 = (pred[768]{0:T(1024)(128)(4,1)S(1)}, pred[768]{0:T(1024)(128)(4,1)}, u32[]{:S(2)}) copy-start(pred[768]{0:T(1024)(128)(4,1)} %get-tuple-element.182) | copy-start | bytes 2308
  256.7 11.4 %copy-start.5 = (s32[256]{0:T(256)S(1)}, s32[256]{0:T(256)}, u32[]{:S(2)}) copy-start(s32[256]{0:T(256)} %iota_add_fusion.3) | copy-start | bytes 3076
  278.1 81.7 %reduce-scatter.5.cloned.1.call-start = ((), (), s32[]{:S(2)}) async-start(), calls=%async_computation.5 | async-start | bytes 2621440 | tf_op jit(solution)/shard_map/reduce_scatter | solution.py:169
Sparse Core Ops, SparseCore 0:
  278.2 41.3 reduce-scatter.2
  322.3 37.4 reduce-scatter.4
where the time goes:
time: 370 us; the launch traced here: 369 us
  waiting for transfers between devices  137 us (37%)
  Pallas kernels  91 us (25%)
  matrix products  53.3 us (14%)
  local copies, waits for them, and re-layouts  40 us (11%)
  starting transfers between devices  22.3 us (6%)
  between operations  13.5 us (4%)
  other arithmetic  11.5 us (3%)
    pallas_call x8, Pallas kernels, cross_spectra(): pl.pallas_call(cross_kernel, grid_spec=grid_spec, out_shape=jax.ShapeDtyp...  91 us
    all_to_all x4, waiting for transfers between devices, exchange(): lax.all_to_all(piece, 'chan', split_axis=0, concat_axis=0, tiled=True)  77.4 us
    reduce_scatter x2, waiting for transfers between devices, finish(): return lax.psum_scatter(lagged, 'tm', scatter_dimension=0, tiled=True)  59.7 us
    dot_general x4, matrix products, accumulate(): spectra = jnp.einsum('asuc,auj->scj', turned, table, precision=FAST)  29.2 us
    all_to_all x4, starting transfers between devices, exchange(): lax.all_to_all(piece, 'chan', split_axis=0, concat_axis=0, tiled=True)  22.2 us
    dot_general x2, matrix products, finish(): lagged = jnp.einsum('kcr,rl->klc', crossed, inverse_cat, precision=FAST)  20.3 us
    transpose x4, local copies, waits for them, and re-layouts, windows(): jnp.concatenate([before, blocks, after], axis=3).transpose(2, 0, 1, 3)  14 us
    while x6, local copies, waits for them, and re-layouts  8.71 us
  transfers between devices with their start and end apart: 6, of which 6 were waited for; matrix products, arithmetic and copies ran while one was open for 12% of the time, Pallas kernels for 22%

commit v1 on v0

--- a/solution.py
+++ b/solution.py
@@ -166,7 +166,8 @@
 
     def finish(crossed):
         lagged = jnp.einsum("kcr,rl->klc", crossed, inverse_cat, precision=FAST)
-        return lax.psum_scatter(lagged, "tm", scatter_dimension=0, tiled=True)
+        parts = lax.all_to_all(lagged, "tm", split_axis=0, concat_axis=0, tiled=True)
+        return jnp.sum(parts, axis=0, keepdims=True)
 
     first = finish(even)
     second = finish(odd)

time: 370 us -> 343 us (0.927)
  waiting for transfers between devices: 137 us -> 107 us
  starting transfers between devices: 22.3 us -> 38.4 us
  between operations: 13.5 us -> 0.13 us
    reduce_scatter x2 -> x0, waiting for transfers between devices: 59.7 us -> none  [finish(): return lax.psum_scatter(lagged, 'tm', scatter_dimension=0, tiled=True)]
    all_to_all x0 -> x2, waiting for transfers between devices: none -> 31 us  [finish(): lax.all_to_all(lagged, 'tm', split_axis=0, concat_axis=0, tiled=True)]
    all_to_all x0 -> x2, starting transfers between devices: none -> 14.2 us  [finish(): lax.all_to_all(lagged, 'tm', split_axis=0, concat_axis=0, tiled=True)]
  transfers between devices with their start and end apart: 6 -> 6, of which waited for: 6 -> 6; matrix products, arithmetic and copies ran while one was open for 12% -> 13% of each run, Pallas kernels for 22% -> 23%
where the time goes in v1:
time: 343 us; the launch traced here: 341 us
  waiting for transfers between devices  107 us (31%)
  Pallas kernels  90.8 us (26%)
  matrix products  52.8 us (15%)
  local copies, waits for them, and re-layouts  40 us (12%)
  starting transfers between devices  38.4 us (11%)
  other arithmetic  12.4 us (4%)
    pallas_call x8, Pallas kernels, cross_spectra(): pl.pallas_call(cross_kernel, grid_spec=grid_spec, out_shape=jax.ShapeDtyp...  90.8 us
    all_to_all x4, waiting for transfers between devices, exchange(): lax.all_to_all(piece, 'chan', split_axis=0, concat_axis=0, tiled=True)  75.8 us
    all_to_all x2, waiting for transfers between devices, finish(): lax.all_to_all(lagged, 'tm', split_axis=0, concat_axis=0, tiled=True)  31 us
    dot_general x4, matrix products, accumulate(): spectra = jnp.einsum('asuc,auj->scj', turned, table, precision=FAST)  29.3 us
    all_to_all x4, starting transfers between devices, exchange(): lax.all_to_all(piece, 'chan', split_axis=0, concat_axis=0, tiled=True)  24.2 us
    dot_general x2, matrix products, finish(): lagged = jnp.einsum('kcr,rl->klc', crossed, inverse_cat, precision=FAST)  19.9 us
    all_to_all x2, starting transfers between devices, finish(): lax.all_to_all(lagged, 'tm', split_axis=0, concat_axis=0, tiled=True)  14.2 us
    transpose x4, local copies, waits for them, and re-layouts, windows(): jnp.concatenate([before, blocks, after], axis=3).transpose(2, 0, 1, 3)  14 us
  transfers between devices with their start and end apart: 6, of which 6 were waited for; matrix products, arithmetic and copies ran while one was open for 13% of the time, Pallas kernels for 23%

profile of v1, /device:TPU:1, one launch (start us, length us, event | category | flops | bytes accessed | tf_op | source)
XLA Modules:
  0.0 341.3 jit_solution(6414201547862915800)
XLA Ops:
  0.0 1.6 slice-done
  1.6 1.2 copy.27
  3.8 3.5 %copy.19 = f32[32,4,8,768]{3,2,1,0:T(8,128)} copy(f32[32,4,8,768]{3,0,2,1:T(8,128)S(1)} %fusion.5) | data formatting | bytes 6291456 | tf_op jit(solution)/shard_map/transpose | solution.py:130
  7.3 10.2 %all-to-all-start.1 = ((f32[32,4,8,768]{3,2,1,0:T(8,128)}), f32[32,4,8,768]{3,2,1,0:T(8,128)}, u32[]{:S(2)}, u32[]{:S(2)}) async-start(f32[32,4,8,768]{3,2,1,0:T(8,128)} %copy.19), calls=%async_computation.1 | async-start | bytes 6291456 | tf_op jit(solution)/shard_map/all_to_all | solution.py:152
  20.1 5.7 %select_reduce_fusion = f32[256,256]{1,0:T(8,128)S(1)} fusion(f32[64]{0:T(128)S(1)} %copy-done.6, s32[256,256]{1,0:T(8,128)S(1)} %iota_subtract_fusion), kind=kLoop, calls=%fused_computation.9 | loop fusion | flops 12517376 | bytes 524544 | tf_op jit(solution)/shard_map/reduce_sum | solution.py:24
  25.9 3.6 %fusion.17 = f32[32,8,512]{2,1,0:T(8,128)} fusion(f32[256,256]{1,0:T(8,128)S(1)} %select_reduce_fusion, s32[512]{0:T(512)S(1)} %iota_add_fusion.2, pred[512]{0:T(512)(128)(4,1)S(1)} %iota_compare_fusion.5), kind=kOutput, calls=%fused_computation.39 | convolution fusion | flops 404750336 | bytes 788992 | tf_op jit(solution)/shard_map/dot_general | solution.py:138
  29.5 35.6 %all-to-all-done.1 = f32[32,4,8,768]{3,2,1,0:T(8,128)} async-done(((f32[32,4,8,768]{3,2,1,0:T(8,128)}), f32[32,4,8,768]{3,2,1,0:T(8,128)}, u32[]{:S(2)}, u32[]{:S(2)}) %all-to-all-start.1) | async-done | bytes 3145760 | tf_op jit(solution)/shard_map/all_to_all | solution.py:152
  65.0 3.2 broadcast.70
  68.2 3.1 broadcast.70.clone
  71.3 171.6 %while.17 = (s32[]{:T(128)}, f32[32,4,8,768]{3,2,1,0:T(8,128)}, f32[4,512,768]{2,1,0:T(8,128)}, f32[4,512,768]{2,1,0:T(8,128)}, f32[16,8,16384]{2,1,0:T(8,128)},...) while((s32[]{:T(128)}, f32[32,4,8,768]{3,2,1,0:T(8,128)}, ...), condition=%wide.region_2.3_spmd, body=%wide.region_1.2_spmd.sunk | while | flops 2419064832 | bytes 58196168 | solution.py:164
  71.3 1.7 constant_dynamic-slice_fusion.2
  73.1 1.2 copy.30
  75.3 3.5 %copy.31 = f32[32,4,8,768]{3,2,1,0:T(8,128)} copy(f32[32,4,8,768]{3,0,2,1:T(8,128)S(1)} %fusion.70) | data formatting | bytes 6291456 | tf_op jit(solution)/shard_map/while/body/eval_jaxpr/transpose | solution.py:130
  78.8 4.1 %all-to-all-start = ((f32[32,4,8,768]{3,2,1,0:T(8,128)}), f32[32,4,8,768]{3,2,1,0:T(8,128)S(1)}, u32[]{:S(2)}, u32[]{:S(2)}) async-start(f32[32,4,8,768]{3,2,1,0:T(8,128)} %copy.31), calls=%async_computation | async-start | bytes 6291456 | tf_op jit(solution)/shard_map/while/body/eval_jaxpr/all_to_all | solution.py:152
  82.9 7.3 %convolution_bitcast_fusion.5.spec_ref = f32[4,768,512]{2,1,0:T(8,128)} fusion(f32[32,4,8,768]{3,2,1,0:T(8,128)} %get-tuple-element.253, f32[32,8,512]{2,1,0:T(8,128)} %get-tuple-element.269), kind=kOutput, calls=%fused_computation.5.clone.1 | convolution fusion | flops 2415919104 | bytes 9961472 | tf_op jit(solution)/shard_map/while/body/eval_jaxpr/asuc,auj->scj/dot_general | solution.py:155
  90.2 11.4 %eval_jaxpr.10 = f32[4,512,768]{2,1,0:T(8,128)} custom-call(s32[4]{0:T(128)S(1)} %get-tuple-element.270.offs_ref, f32[4,768,512]{2,1,0:T(8,128)} %convolution_bitcast_fusion.5.spec_ref, f32[4,512,768]{2,1,0:T(8,128)} %get-tuple-element.254.acc_ref), custom_call_target="tpu_custom_call", output_to_operand_aliasing={{}: (2, {})} | custom-call | tf_op jit(solution)/shard_map/while/body/eval_jaxpr/pallas_call | solution.py:114
  101.5 11.3 %eval_jaxpr.11 = f32[4,512,768]{2,1,0:T(8,128)} custom-call(s32[4]{0:T(128)S(1)} %get-tuple-element.271.offs_ref, f32[4,768,512]{2,1,0:T(8,128)} %convolution_bitcast_fusion.5.spec_ref, f32[4,512,768]{2,1,0:T(8,128)} %get-tuple-element.255.acc_ref), custom_call_target="tpu_custom_call", output_to_operand_aliasing={{}: (2, {})} | custom-call | tf_op jit(solution)/shard_map/while/body/eval_jaxpr/pallas_call | solution.py:114
  112.9 14.3 %all-to-all-done = f32[32,4,8,768]{3,2,1,0:T(8,128)S(1)} async-done(((f32[32,4,8,768]{3,2,1,0:T(8,128)}), f32[32,4,8,768]{3,2,1,0:T(8,128)S(1)}, u32[]{:S(2)}, u32[]{:S(2)}) %all-to-all-start) | async-done | bytes 3145760 | tf_op jit(solution)/shard_map/while/body/eval_jaxpr/all_to_all | solution.py:152
  127.2 1.7 copy.43
  128.9 1.7 constant_dynamic-slice_fusion.2
  130.6 1.2 copy.30
  132.8 3.5 %copy.31 = f32[32,4,8,768]{3,2,1,0:T(8,128)} copy(f32[32,4,8,768]{3,0,2,1:T(8,128)S(1)} %fusion.70) | data formatting | bytes 6291456 | tf_op jit(solution)/shard_map/while/body/eval_jaxpr/transpose | solution.py:130
  136.3 4.1 %all-to-all-start = ((f32[32,4,8,768]{3,2,1,0:T(8,128)}), f32[32,4,8,768]{3,2,1,0:T(8,128)S(1)}, u32[]{:S(2)}, u32[]{:S(2)}) async-start(f32[32,4,8,768]{3,2,1,0:T(8,128)} %copy.31), calls=%async_computation | async-start | bytes 6291456 | tf_op jit(solution)/shard_map/while/body/eval_jaxpr/all_to_all | solution.py:152
  140.4 7.3 %convolution_bitcast_fusion.5.spec_ref = f32[4,768,512]{2,1,0:T(8,128)} fusion(f32[32,4,8,768]{3,2,1,0:T(8,128)} %get-tuple-element.253, f32[32,8,512]{2,1,0:T(8,128)} %get-tuple-element.269), kind=kOutput, calls=%fused_computation.5.clone.1 | convolution fusion | flops 2415919104 | bytes 9961472 | tf_op jit(solution)/shard_map/while/body/eval_jaxpr/asuc,auj->scj/dot_general | solution.py:155
  147.7 11.4 %eval_jaxpr.10 = f32[4,512,768]{2,1,0:T(8,128)} custom-call(s32[4]{0:T(128)S(1)} %get-tuple-element.270.offs_ref, f32[4,768,512]{2,1,0:T(8,128)} %convolution_bitcast_fusion.5.spec_ref, f32[4,512,768]{2,1,0:T(8,128)} %get-tuple-element.254.acc_ref), custom_call_target="tpu_custom_call", output_to_operand_aliasing={{}: (2, {})} | custom-call | tf_op jit(solution)/shard_map/while/body/eval_jaxpr/pallas_call | solution.py:114
  159.1 11.3 %eval_jaxpr.11 = f32[4,512,768]{2,1,0:T(8,128)} custom-call(s32[4]{0:T(128)S(1)} %get-tuple-element.271.offs_ref, f32[4,768,512]{2,1,0:T(8,128)} %convolution_bitcast_fusion.5.spec_ref, f32[4,512,768]{2,1,0:T(8,128)} %get-tuple-element.255.acc_ref), custom_call_target="tpu_custom_call", output_to_operand_aliasing={{}: (2, {})} | custom-call | tf_op jit(solution)/shard_map/while/body/eval_jaxpr/pallas_call | solution.py:114
  170.4 12.5 %all-to-all-done = f32[32,4,8,768]{3,2,1,0:T(8,128)S(1)} async-done(((f32[32,4,8,768]{3,2,1,0:T(8,128)}), f32[32,4,8,768]{3,2,1,0:T(8,128)S(1)}, u32[]{:S(2)}, u32[]{:S(2)}) %all-to-all-start) | async-done | bytes 3145760 | tf_op jit(solution)/shard_map/while/body/eval_jaxpr/all_to_all | solution.py:152
  182.9 1.7 copy.43
  184.6 1.7 constant_dynamic-slice_fusion.2
  186.3 1.2 copy.30
  188.5 3.5 %copy.31 = f32[32,4,8,768]{3,2,1,0:T(8,128)} copy(f32[32,4,8,768]{3,0,2,1:T(8,128)S(1)} %fusion.70) | data formatting | bytes 6291456 | tf_op jit(solution)/shard_map/while/body/eval_jaxpr/transpose | solution.py:130
  192.0 5.8 %all-to-all-start = ((f32[32,4,8,768]{3,2,1,0:T(8,128)}), f32[32,4,8,768]{3,2,1,0:T(8,128)S(1)}, u32[]{:S(2)}, u32[]{:S(2)}) async-start(f32[32,4,8,768]{3,2,1,0:T(8,128)} %copy.31), calls=%async_computation | async-start | bytes 6291456 | tf_op jit(solution)/shard_map/while/body/eval_jaxpr/all_to_all | solution.py:152
  197.8 7.3 %convolution_bitcast_fusion.5.spec_ref = f32[4,768,512]{2,1,0:T(8,128)} fusion(f32[32,4,8,768]{3,2,1,0:T(8,128)} %get-tuple-element.253, f32[32,8,512]{2,1,0:T(8,128)} %get-tuple-element.269), kind=kOutput, calls=%fused_computation.5.clone.1 | convolution fusion | flops 2415919104 | bytes 9961472 | tf_op jit(solution)/shard_map/while/body/eval_jaxpr/asuc,auj->scj/dot_general | solution.py:155
  205.2 11.4 %eval_jaxpr.10 = f32[4,512,768]{2,1,0:T(8,128)} custom-call(s32[4]{0:T(128)S(1)} %get-tuple-element.270.offs_ref, f32[4,768,512]{2,1,0:T(8,128)} %convolution_bitcast_fusion.5.spec_ref, f32[4,512,768]{2,1,0:T(8,128)} %get-tuple-element.254.acc_ref), custom_call_target="tpu_custom_call", output_to_operand_aliasing={{}: (2, {})} | custom-call | tf_op jit(solution)/shard_map/while/body/eval_jaxpr/pallas_call | solution.py:114
  216.5 11.3 %eval_jaxpr.11 = f32[4,512,768]{2,1,0:T(8,128)} custom-call(s32[4]{0:T(128)S(1)} %get-tuple-element.271.offs_ref, f32[4,768,512]{2,1,0:T(8,128)} %convolution_bitcast_fusion.5.spec_ref, f32[4,512,768]{2,1,0:T(8,128)} %get-tuple-element.255.acc_ref), custom_call_target="tpu_custom_call", output_to_operand_aliasing={{}: (2, {})} | custom-call | tf_op jit(solution)/shard_map/while/body/eval_jaxpr/pallas_call | solution.py:114
  227.9 13.4 %all-to-all-done = f32[32,4,8,768]{3,2,1,0:T(8,128)S(1)} async-done(((f32[32,4,8,768]{3,2,1,0:T(8,128)}), f32[32,4,8,768]{3,2,1,0:T(8,128)S(1)}, u32[]{:S(2)}, u32[]{:S(2)}) %all-to-all-start) | async-done | bytes 3145760 | tf_op jit(solution)/shard_map/while/body/eval_jaxpr/all_to_all | solution.py:152
  241.3 1.7 copy.43
  243.0 7.3 %convolution_bitcast_fusion.1.spec_ref = f32[4,768,512]{2,1,0:T(8,128)} fusion(f32[32,4,8,768]{3,2,1,0:T(8,128)} %get-tuple-element.136, f32[32,8,512]{2,1,0:T(8,128)} %get-tuple-element.286), kind=kOutput, calls=%fused_computation.16 | convolution fusion | flops 2415919104 | bytes 9961472 | tf_op jit(solution)/shard_map/asuc,auj->scj/dot_general | solution.py:155
  250.3 11.4 %shard_map.37 = f32[4,512,768]{2,1,0:T(8,128)} custom-call(s32[4]{0:T(128)S(1)} %get-tuple-element.285, f32[4,768,512]{2,1,0:T(8,128)} %convolution_bitcast_fusion.1.spec_ref, f32[4,512,768]{2,1,0:T(8,128)} %get-tuple-element.137.acc_ref), custom_call_target="tpu_custom_call", output_to_operand_aliasing={{}: (2, {})} | custom-call | tf_op jit(solution)/shard_map/pallas_call | solution.py:114
  261.7 10.0 %convolution_bitcast_fusion.3 = f32[4,256,512]{2,1,0:T(8,128)} fusion(f32[4,512,768]{2,1,0:T(8,128)} %shard_map.37, s32[256]{0:T(256)S(1)} %copy-done.5, s32[768]{0:T(1024)S(1)} %copy-done.1, s32[768]{0:T(1024)S(1)} %copy-done.2, f32[768]{0:T(1024)S(1)} %copy-done, pred[768]{0:T(1024)(128)(4,1)S(1)} %copy-done.3, pred[768]{0:T(1024)(128)(4,1)S(1)} %copy-done.4), kind=kOutput, calls=%fused_computation.19 | convolution fusion | flops 2420244480 | bytes 8400384 | tf_op jit(solution)/shard_map/kcr,rl->klc/dot_general | solution.py:168
  271.7 8.8 %all-to-all-start.2 = ((f32[4,256,512]{2,1,0:T(8,128)}), f32[4,256,512]{2,1,0:T(8,128)S(1)}, u32[]{:S(2)}, u32[]{:S(2)}) async-start(f32[4,256,512]{2,1,0:T(8,128)} %convolution_bitcast_fusion.3), calls=%async_computation.2 | async-start | bytes 4194304 | tf_op jit(solution)/shard_map/all_to_all | solution.py:169
  280.5 11.3 %shard_map.38 = f32[4,512,768]{2,1,0:T(8,128)} custom-call(s32[4]{0:T(128)S(1)} %get-tuple-element.284, f32[4,768,512]{2,1,0:T(8,128)} %convolution_bitcast_fusion.1.spec_ref, f32[4,512,768]{2,1,0:T(8,128)} %get-tuple-element.138.acc_ref), custom_call_target="tpu_custom_call", output_to_operand_aliasing={{}: (2, {})} | custom-call | tf_op jit(solution)/shard_map/pallas_call | solution.py:114
  291.8 9.9 %convolution_bitcast_fusion.2 = f32[4,256,512]{2,1,0:T(8,128)} fusion(f32[4,512,768]{2,1,0:T(8,128)} %shard_map.38, s32[256]{0:T(256)S(1)} %copy-done.5, s32[768]{0:T(1024)S(1)} %copy-done.1, s32[768]{0:T(1024)S(1)} %copy-done.2, f32[768]{0:T(1024)S(1)} %copy-done, pred[768]{0:T(1024)(128)(4,1)S(1)} %copy-done.3, pred[768]{0:T(1024)(128)(4,1)S(1)} %copy-done.4), kind=kOutput, calls=%fused_computation.18 | convolution fusion | flops 2420244480 | bytes 8400384 | tf_op jit(solution)/shard_map/kcr,rl->klc/dot_general | solution.py:168
  301.8 4.9 %all-to-all-done.2 = f32[4,256,512]{2,1,0:T(8,128)S(1)} async-done(((f32[4,256,512]{2,1,0:T(8,128)}), f32[4,256,512]{2,1,0:T(8,128)S(1)}, u32[]{:S(2)}, u32[]{:S(2)}) %all-to-all-start.2) | async-done | bytes 2097184 | tf_op jit(solution)/shard_map/all_to_all | solution.py:169
  306.7 5.4 %all-to-all-start.3 = ((f32[4,256,512]{2,1,0:T(8,128)}), f32[4,256,512]{2,1,0:T(8,128)}, u32[]{:S(2)}, u32[]{:S(2)}) async-start(f32[4,256,512]{2,1,0:T(8,128)} %convolution_bitcast_fusion.2), calls=%async_computation.3 | async-start | bytes 4194304 | tf_op jit(solution)/shard_map/all_to_all | solution.py:169
  312.3 26.1 %all-to-all-done.3 = f32[4,256,512]{2,1,0:T(8,128)} async-done(((f32[4,256,512]{2,1,0:T(8,128)}), f32[4,256,512]{2,1,0:T(8,128)}, u32[]{:S(2)}, u32[]{:S(2)}) %all-to-all-start.3) | async-done | bytes 2097184 | tf_op jit(solution)/shard_map/all_to_all | solution.py:169
  338.4 1.9 reduce_sum.29
  340.3 1.0 pad_maximum_fusion.4
  (39 shorter events, 6.8 us)
Async XLA Ops:
  0.0 1.6 slice-start
  7.3 10.2 %copy-start.7 = (s32[8]{0:T(128)S(1)}, s32[8]{0:T(128)}, u32[]{:S(2)}) copy-start(s32[8]{0:T(128)} %param.7) | copy-start | bytes 100
  7.3 12.8 %copy-start.6 = (f32[64]{0:T(128)S(1)}, f32[64]{0:T(128)}, u32[]{:S(2)}) copy-start(f32[64]{0:T(128)} %param.6) | copy-start | bytes 772
  7.3 57.7 %all-to-all-start.1 = ((f32[32,4,8,768]{3,2,1,0:T(8,128)}), f32[32,4,8,768]{3,2,1,0:T(8,128)}, u32[]{:S(2)}, u32[]{:S(2)}) async-start(f32[32,4,8,768]{3,2,1,0:T(8,128)} %copy.19), calls=%async_computation.1 | async-start | bytes 6291456 | tf_op jit(solution)/shard_map/all_to_all | solution.py:152
  78.8 48.4 %all-to-all-start = ((f32[32,4,8,768]{3,2,1,0:T(8,128)}), f32[32,4,8,768]{3,2,1,0:T(8,128)S(1)}, u32[]{:S(2)}, u32[]{:S(2)}) async-start(f32[32,4,8,768]{3,2,1,0:T(8,128)} %copy.31), calls=%async_computation | async-start | bytes 6291456 | tf_op jit(solution)/shard_map/while/body/eval_jaxpr/all_to_all | solution.py:152
  136.3 46.6 %all-to-all-start = ((f32[32,4,8,768]{3,2,1,0:T(8,128)}), f32[32,4,8,768]{3,2,1,0:T(8,128)S(1)}, u32[]{:S(2)}, u32[]{:S(2)}) async-start(f32[32,4,8,768]{3,2,1,0:T(8,128)} %copy.31), calls=%async_computation | async-start | bytes 6291456 | tf_op jit(solution)/shard_map/while/body/eval_jaxpr/all_to_all | solution.py:152
  192.0 49.3 %all-to-all-start = ((f32[32,4,8,768]{3,2,1,0:T(8,128)}), f32[32,4,8,768]{3,2,1,0:T(8,128)S(1)}, u32[]{:S(2)}, u32[]{:S(2)}) async-start(f32[32,4,8,768]{3,2,1,0:T(8,128)} %copy.31), calls=%async_computation | async-start | bytes 6291456 | tf_op jit(solution)/shard_map/while/body/eval_jaxpr/all_to_all | solution.py:152
  250.3 11.4 %copy-start = (f32[768]{0:T(1024)S(1)}, f32[768]{0:T(1024)}, u32[]{:S(2)}) copy-start(f32[768]{0:T(1024)} %fusion.34) | copy-start | bytes 9220
  250.3 11.4 %copy-start.1 = (s32[768]{0:T(1024)S(1)}, s32[768]{0:T(1024)}, u32[]{:S(2)}) copy-start(s32[768]{0:T(1024)} %get-tuple-element.179) | copy-start | bytes 9220
  250.3 11.4 %copy-start.2 = (s32[768]{0:T(1024)S(1)}, s32[768]{0:T(1024)}, u32[]{:S(2)}) copy-start(s32[768]{0:T(1024)} %get-tuple-element.180) | copy-start | bytes 9220
  250.3 11.4 %copy-start.3 = (pred[768]{0:T(1024)(128)(4,1)S(1)}, pred[768]{0:T(1024)(128)(4,1)}, u32[]{:S(2)}) copy-start(pred[768]{0:T(1024)(128)(4,1)} %get-tuple-element.181) | copy-start | bytes 2308
  250.3 11.4 %copy-start.4 = (pred[768]{0:T(1024)(128)(4,1)S(1)}, pred[768]{0:T(1024)(128)(4,1)}, u32[]{:S(2)}) copy-start(pred[768]{0:T(1024)(128)(4,1)} %get-tuple-element.182) | copy-start | bytes 2308
  250.3 11.4 %copy-start.5 = (s32[256]{0:T(256)S(1)}, s32[256]{0:T(256)}, u32[]{:S(2)}) copy-start(s32[256]{0:T(256)} %iota_add_fusion.3) | copy-start | bytes 3076
  271.7 35.0 %all-to-all-start.2 = ((f32[4,256,512]{2,1,0:T(8,128)}), f32[4,256,512]{2,1,0:T(8,128)S(1)}, u32[]{:S(2)}, u32[]{:S(2)}) async-start(f32[4,256,512]{2,1,0:T(8,128)} %convolution_bitcast_fusion.3), calls=%async_computation.2 | async-start | bytes 4194304 | tf_op jit(solution)/shard_map/all_to_all | solution.py:169
  306.7 31.7 %all-to-all-start.3 = ((f32[4,256,512]{2,1,0:T(8,128)}), f32[4,256,512]{2,1,0:T(8,128)}, u32[]{:S(2)}, u32[]{:S(2)}) async-start(f32[4,256,512]{2,1,0:T(8,128)} %convolution_bitcast_fusion.2), calls=%async_computation.3 | async-start | bytes 4194304 | tf_op jit(solution)/shard_map/all_to_all | solution.py:169

commit v2 on v1

--- a/solution.py
+++ b/solution.py
@@ -62,7 +62,7 @@
     return jnp.concatenate([before, array, after], axis=dim)
 
 
-CHUNKS = 4
+CHUNKS = 8
 
 
 def cross_kernel(offs_ref, spec_ref, acc_ref, out_ref):

time: 343 us -> 352 us (1.026)
  waiting for transfers between devices: 107 us -> 65.7 us
  Pallas kernels: 90.8 us -> 128 us
  starting transfers between devices: 38.4 us -> 55.6 us
  matrix products: 52.8 us -> 43.8 us
    all_to_all x4 -> x8, waiting for transfers between devices: 75.8 us -> 33 us  [exchange(): lax.all_to_all(piece, 'chan', split_axis=0, concat_axis=0, tiled=True)]
    pallas_call x8 -> x16, Pallas kernels: 90.8 us -> 128 us  [cross_spectra(): pl.pallas_call(cross_kernel, grid_spec=grid_spec, out_shape=jax.ShapeDtyp...]
    all_to_all x4 -> x8, starting transfers between devices: 24.2 us -> 43 us  [exchange(): lax.all_to_all(piece, 'chan', split_axis=0, concat_axis=0, tiled=True)]
    dot_general x4 -> x8, matrix products: 29.3 us -> 20.3 us  [accumulate(): spectra = jnp.einsum('asuc,auj->scj', turned, table, precision=FAST)]
    while x6 -> x14, local copies, waits for them, and re-layouts: 8.69 us -> 5 us
    dynamic_slice x5 -> x9, local copies, waits for them, and re-layouts: 6.77 us -> 10.3 us  [exchange(): lax.dynamic_slice_in_dim(record, g * step, step, 0)]
    transpose x4 -> x8, local copies, waits for them, and re-layouts: 14 us -> 16.8 us  [windows(): jnp.concatenate([before, blocks, after], axis=3).transpose(2, 0, 1, 3)]
  transfers between devices with their start and end apart: 6 -> 10, of which waited for: 6 -> 10; matrix products, arithmetic and copies ran while one was open for 13% -> 12% of each run, Pallas kernels for 23% -> 34%
where the time goes in v2:
time: 352 us; the launch traced here: 349 us
  Pallas kernels  128 us (36%)
  waiting for transfers between devices  65.7 us (19%)
  starting transfers between devices  55.6 us (16%)
  matrix products  43.8 us (12%)
  local copies, waits for them, and re-layouts  43.1 us (12%)
  other arithmetic  12.4 us (4%)
    pallas_call x16, Pallas kernels, cross_spectra(): pl.pallas_call(cross_kernel, grid_spec=grid_spec, out_shape=jax.ShapeDtyp...  128 us
    all_to_all x8, starting transfers between devices, exchange(): lax.all_to_all(piece, 'chan', split_axis=0, concat_axis=0, tiled=True)  43 us
    all_to_all x8, waiting for transfers between devices, exchange(): lax.all_to_all(piece, 'chan', split_axis=0, concat_axis=0, tiled=True)  33 us
    all_to_all x2, waiting for transfers between devices, finish(): lax.all_to_all(lagged, 'tm', split_axis=0, concat_axis=0, tiled=True)  32.7 us
    dot_general x8, matrix products, accumulate(): spectra = jnp.einsum('asuc,auj->scj', turned, table, precision=FAST)  20.3 us
    dot_general x2, matrix products, finish(): lagged = jnp.einsum('kcr,rl->klc', crossed, inverse_cat, precision=FAST)  19.9 us
    transpose x8, local copies, waits for them, and re-layouts, windows(): jnp.concatenate([before, blocks, after], axis=3).transpose(2, 0, 1, 3)  16.8 us
    all_to_all x2, starting transfers between devices, finish(): lax.all_to_all(lagged, 'tm', split_axis=0, concat_axis=0, tiled=True)  12.6 us
  transfers between devices with their start and end apart: 10, of which 10 were waited for; matrix products, arithmetic and copies ran while one was open for 12% of the time, Pallas kernels for 34%

profile of v2, /device:TPU:1, one launch (start us, length us, event | category | flops | bytes accessed | tf_op | source)
XLA Modules:
  0.0 349.5 jit_solution(11460305449643277443)
XLA Ops:
  4.9 10.1 %all-to-all-start.1 = ((f32[32,2,8,768]{3,2,1,0:T(8,128)}), f32[32,2,8,768]{3,2,1,0:T(8,128)S(1)}, u32[]{:S(2)}, u32[]{:S(2)}) async-start(f32[32,2,8,768]{3,2,1,0:T(8,128)} %copy.19), calls=%async_computation.1 | async-start | bytes 3145728 | tf_op jit(solution)/shard_map/all_to_all | solution.py:152
  17.5 5.7 %select_reduce_fusion = f32[256,256]{1,0:T(8,128)S(1)} fusion(f32[64]{0:T(128)S(1)} %copy-done.7, s32[256,256]{1,0:T(8,128)S(1)} %iota_subtract_fusion), kind=kLoop, calls=%fused_computation.9 | loop fusion | flops 12517376 | bytes 524544 | tf_op jit(solution)/shard_map/reduce_sum | solution.py:24
  23.2 3.6 %fusion.17 = f32[32,8,512]{2,1,0:T(8,128)} fusion(f32[256,256]{1,0:T(8,128)S(1)} %select_reduce_fusion, s32[512]{0:T(512)S(1)} %iota_add_fusion.2, pred[512]{0:T(512)(128)(4,1)S(1)} %iota_compare_fusion.5), kind=kOutput, calls=%fused_computation.39 | convolution fusion | flops 404750336 | bytes 788992 | tf_op jit(solution)/shard_map/dot_general | solution.py:138
  26.8 12.4 %all-to-all-done.1 = f32[32,2,8,768]{3,2,1,0:T(8,128)S(1)} async-done(((f32[32,2,8,768]{3,2,1,0:T(8,128)}), f32[32,2,8,768]{3,2,1,0:T(8,128)S(1)}, u32[]{:S(2)}, u32[]{:S(2)}) %all-to-all-start.1) | async-done | bytes 1572896 | tf_op jit(solution)/shard_map/all_to_all | solution.py:152
  39.2 3.2 broadcast.70
  42.4 3.2 broadcast.70.clone
  45.6 215.3 %while.17 = (s32[]{:T(128)}, f32[32,2,8,768]{3,2,1,0:T(8,128)S(1)}, f32[4,512,768]{2,1,0:T(8,128)}, f32[4,512,768]{2,1,0:T(8,128)}, f32[16,8,16384]{2,1,0:T(8,12...) while((s32[]{:T(128)}, f32[32,2,8,768]{3,2,1,0:T(8,128)S(1)}, ...), condition=%wide.region_2.3_spmd, body=%wide.region_1.2_spmd.sunk | while | flops 1209532416 | bytes 29360328 | solution.py:164
  50.0 4.0 %all-to-all-start = ((f32[32,2,8,768]{3,2,1,0:T(8,128)}), f32[32,2,8,768]{3,2,1,0:T(8,128)S(1)}, u32[]{:S(2)}, u32[]{:S(2)}) async-start(f32[32,2,8,768]{3,2,1,0:T(8,128)} %copy.31), calls=%async_computation | async-start | bytes 3145728 | tf_op jit(solution)/shard_map/while/body/eval_jaxpr/all_to_all | solution.py:152
  54.0 2.5 convolution_bitcast_fusion.5.spec_ref
  56.5 8.0 %eval_jaxpr.10 = f32[4,512,768]{2,1,0:T(8,128)} custom-call(s32[4]{0:T(128)S(1)} %get-tuple-element.270.offs_ref, f32[2,768,512]{2,1,0:T(8,128)S(1)} %convolution_bitcast_fusion.5.spec_ref, f32[4,512,768]{2,1,0:T(8,128)} %get-tuple-element.254.acc_ref), custom_call_target="tpu_custom_call", output_to_operand_aliasing={{}: (2, {})} | custom-call | tf_op jit(solution)/shard_map/while/body/eval_jaxpr/pallas_call | solution.py:114
  64.5 8.0 %eval_jaxpr.11 = f32[4,512,768]{2,1,0:T(8,128)} custom-call(s32[4]{0:T(128)S(1)} %get-tuple-element.271.offs_ref, f32[2,768,512]{2,1,0:T(8,128)S(1)} %convolution_bitcast_fusion.5.spec_ref, f32[4,512,768]{2,1,0:T(8,128)} %get-tuple-element.255.acc_ref), custom_call_target="tpu_custom_call", output_to_operand_aliasing={{}: (2, {})} | custom-call | tf_op jit(solution)/shard_map/while/body/eval_jaxpr/pallas_call | solution.py:114
  72.5 3.4 all-to-all-done
  80.5 4.4 %all-to-all-start = ((f32[32,2,8,768]{3,2,1,0:T(8,128)}), f32[32,2,8,768]{3,2,1,0:T(8,128)S(1)}, u32[]{:S(2)}, u32[]{:S(2)}) async-start(f32[32,2,8,768]{3,2,1,0:T(8,128)} %copy.31), calls=%async_computation | async-start | bytes 3145728 | tf_op jit(solution)/shard_map/while/body/eval_jaxpr/all_to_all | solution.py:152
  84.8 2.5 convolution_bitcast_fusion.5.spec_ref
  87.3 8.0 %eval_jaxpr.10 = f32[4,512,768]{2,1,0:T(8,128)} custom-call(s32[4]{0:T(128)S(1)} %get-tuple-element.270.offs_ref, f32[2,768,512]{2,1,0:T(8,128)S(1)} %convolution_bitcast_fusion.5.spec_ref, f32[4,512,768]{2,1,0:T(8,128)} %get-tuple-element.254.acc_ref), custom_call_target="tpu_custom_call", output_to_operand_aliasing={{}: (2, {})} | custom-call | tf_op jit(solution)/shard_map/while/body/eval_jaxpr/pallas_call | solution.py:114
  95.3 8.0 %eval_jaxpr.11 = f32[4,512,768]{2,1,0:T(8,128)} custom-call(s32[4]{0:T(128)S(1)} %get-tuple-element.271.offs_ref, f32[2,768,512]{2,1,0:T(8,128)S(1)} %convolution_bitcast_fusion.5.spec_ref, f32[4,512,768]{2,1,0:T(8,128)} %get-tuple-element.255.acc_ref), custom_call_target="tpu_custom_call", output_to_operand_aliasing={{}: (2, {})} | custom-call | tf_op jit(solution)/shard_map/while/body/eval_jaxpr/pallas_call | solution.py:114
  103.3 3.3 all-to-all-done
  111.2 4.4 %all-to-all-start = ((f32[32,2,8,768]{3,2,1,0:T(8,128)}), f32[32,2,8,768]{3,2,1,0:T(8,128)S(1)}, u32[]{:S(2)}, u32[]{:S(2)}) async-start(f32[32,2,8,768]{3,2,1,0:T(8,128)} %copy.31), calls=%async_computation | async-start | bytes 3145728 | tf_op jit(solution)/shard_map/while/body/eval_jaxpr/all_to_all | solution.py:152
  118.1 8.0 %eval_jaxpr.10 = f32[4,512,768]{2,1,0:T(8,128)} custom-call(s32[4]{0:T(128)S(1)} %get-tuple-element.270.offs_ref, f32[2,768,512]{2,1,0:T(8,128)S(1)} %convolution_bitcast_fusion.5.spec_ref, f32[4,512,768]{2,1,0:T(8,128)} %get-tuple-element.254.acc_ref), custom_call_target="tpu_custom_call", output_to_operand_aliasing={{}: (2, {})} | custom-call | tf_op jit(solution)/shard_map/while/body/eval_jaxpr/pallas_call | solution.py:114
  126.2 8.0 %eval_jaxpr.11 = f32[4,512,768]{2,1,0:T(8,128)} custom-call(s32[4]{0:T(128)S(1)} %get-tuple-element.271.offs_ref, f32[2,768,512]{2,1,0:T(8,128)S(1)} %convolution_bitcast_fusion.5.spec_ref, f32[4,512,768]{2,1,0:T(8,128)} %get-tuple-element.255.acc_ref), custom_call_target="tpu_custom_call", output_to_operand_aliasing={{}: (2, {})} | custom-call | tf_op jit(solution)/shard_map/while/body/eval_jaxpr/pallas_call | solution.py:114
  134.1 2.6 all-to-all-done
  141.4 5.1 %all-to-all-start = ((f32[32,2,8,768]{3,2,1,0:T(8,128)}), f32[32,2,8,768]{3,2,1,0:T(8,128)S(1)}, u32[]{:S(2)}, u32[]{:S(2)}) async-start(f32[32,2,8,768]{3,2,1,0:T(8,128)} %copy.31), calls=%async_computation | async-start | bytes 3145728 | tf_op jit(solution)/shard_map/while/body/eval_jaxpr/all_to_all | solution.py:152
  146.5 2.5 convolution_bitcast_fusion.5.spec_ref
  149.0 8.0 %eval_jaxpr.10 = f32[4,512,768]{2,1,0:T(8,128)} custom-call(s32[4]{0:T(128)S(1)} %get-tuple-element.270.offs_ref, f32[2,768,512]{2,1,0:T(8,128)S(1)} %convolution_bitcast_fusion.5.spec_ref, f32[4,512,768]{2,1,0:T(8,128)} %get-tuple-element.254.acc_ref), custom_call_target="tpu_custom_call", output_to_operand_aliasing={{}: (2, {})} | custom-call | tf_op jit(solution)/shard_map/while/body/eval_jaxpr/pallas_call | solution.py:114
  157.0 8.0 %eval_jaxpr.11 = f32[4,512,768]{2,1,0:T(8,128)} custom-call(s32[4]{0:T(128)S(1)} %get-tuple-element.271.offs_ref, f32[2,768,512]{2,1,0:T(8,128)S(1)} %convolution_bitcast_fusion.5.spec_ref, f32[4,512,768]{2,1,0:T(8,128)} %get-tuple-element.255.acc_ref), custom_call_target="tpu_custom_call", output_to_operand_aliasing={{}: (2, {})} | custom-call | tf_op jit(solution)/shard_map/while/body/eval_jaxpr/pallas_call | solution.py:114
  165.0 2.7 all-to-all-done
  172.3 5.0 %all-to-all-start = ((f32[32,2,8,768]{3,2,1,0:T(8,128)}), f32[32,2,8,768]{3,2,1,0:T(8,128)S(1)}, u32[]{:S(2)}, u32[]{:S(2)}) async-start(f32[32,2,8,768]{3,2,1,0:T(8,128)} %copy.31), calls=%async_computation | async-start | bytes 3145728 | tf_op jit(solution)/shard_map/while/body/eval_jaxpr/all_to_all | solution.py:152
  179.8 8.0 %eval_jaxpr.10 = f32[4,512,768]{2,1,0:T(8,128)} custom-call(s32[4]{0:T(128)S(1)} %get-tuple-element.270.offs_ref, f32[2,768,512]{2,1,0:T(8,128)S(1)} %convolution_bitcast_fusion.5.spec_ref, f32[4,512,768]{2,1,0:T(8,128)} %get-tuple-element.254.acc_ref), custom_call_target="tpu_custom_call", output_to_operand_aliasing={{}: (2, {})} | custom-call | tf_op jit(solution)/shard_map/while/body/eval_jaxpr/pallas_call | solution.py:114
  187.8 8.0 %eval_jaxpr.11 = f32[4,512,768]{2,1,0:T(8,128)} custom-call(s32[4]{0:T(128)S(1)} %get-tuple-element.271.offs_ref, f32[2,768,512]{2,1,0:T(8,128)S(1)} %convolution_bitcast_fusion.5.spec_ref, f32[4,512,768]{2,1,0:T(8,128)} %get-tuple-element.255.acc_ref), custom_call_target="tpu_custom_call", output_to_operand_aliasing={{}: (2, {})} | custom-call | tf_op jit(solution)/shard_map/while/body/eval_jaxpr/pallas_call | solution.py:114
  195.8 2.7 all-to-all-done
  203.1 5.0 %all-to-all-start = ((f32[32,2,8,768]{3,2,1,0:T(8,128)}), f32[32,2,8,768]{3,2,1,0:T(8,128)S(1)}, u32[]{:S(2)}, u32[]{:S(2)}) async-start(f32[32,2,8,768]{3,2,1,0:T(8,128)} %copy.31), calls=%async_computation | async-start | bytes 3145728 | tf_op jit(solution)/shard_map/while/body/eval_jaxpr/all_to_all | solution.py:152
  208.1 2.5 convolution_bitcast_fusion.5.spec_ref
  210.6 8.0 %eval_jaxpr.10 = f32[4,512,768]{2,1,0:T(8,128)} custom-call(s32[4]{0:T(128)S(1)} %get-tuple-element.270.offs_ref, f32[2,768,512]{2,1,0:T(8,128)S(1)} %convolution_bitcast_fusion.5.spec_ref, f32[4,512,768]{2,1,0:T(8,128)} %get-tuple-element.254.acc_ref), custom_call_target="tpu_custom_call", output_to_operand_aliasing={{}: (2, {})} | custom-call | tf_op jit(solution)/shard_map/while/body/eval_jaxpr/pallas_call | solution.py:114
  218.6 8.0 %eval_jaxpr.11 = f32[4,512,768]{2,1,0:T(8,128)} custom-call(s32[4]{0:T(128)S(1)} %get-tuple-element.271.offs_ref, f32[2,768,512]{2,1,0:T(8,128)S(1)} %convolution_bitcast_fusion.5.spec_ref, f32[4,512,768]{2,1,0:T(8,128)} %get-tuple-element.255.acc_ref), custom_call_target="tpu_custom_call", output_to_operand_aliasing={{}: (2, {})} | custom-call | tf_op jit(solution)/shard_map/while/body/eval_jaxpr/pallas_call | solution.py:114
  226.6 2.8 all-to-all-done
  234.0 4.9 %all-to-all-start = ((f32[32,2,8,768]{3,2,1,0:T(8,128)}), f32[32,2,8,768]{3,2,1,0:T(8,128)S(1)}, u32[]{:S(2)}, u32[]{:S(2)}) async-start(f32[32,2,8,768]{3,2,1,0:T(8,128)} %copy.31), calls=%async_computation | async-start | bytes 3145728 | tf_op jit(solution)/shard_map/while/body/eval_jaxpr/all_to_all | solution.py:152
  241.4 8.0 %eval_jaxpr.10 = f32[4,512,768]{2,1,0:T(8,128)} custom-call(s32[4]{0:T(128)S(1)} %get-tuple-element.270.offs_ref, f32[2,768,512]{2,1,0:T(8,128)S(1)} %convolution_bitcast_fusion.5.spec_ref, f32[4,512,768]{2,1,0:T(8,128)} %get-tuple-element.254.acc_ref), custom_call_target="tpu_custom_call", output_to_operand_aliasing={{}: (2, {})} | custom-call | tf_op jit(solution)/shard_map/while/body/eval_jaxpr/pallas_call | solution.py:114
  249.4 8.0 %eval_jaxpr.11 = f32[4,512,768]{2,1,0:T(8,128)} custom-call(s32[4]{0:T(128)S(1)} %get-tuple-element.271.offs_ref, f32[2,768,512]{2,1,0:T(8,128)S(1)} %convolution_bitcast_fusion.5.spec_ref, f32[4,512,768]{2,1,0:T(8,128)} %get-tuple-element.255.acc_ref), custom_call_target="tpu_custom_call", output_to_operand_aliasing={{}: (2, {})} | custom-call | tf_op jit(solution)/shard_map/while/body/eval_jaxpr/pallas_call | solution.py:114
  257.4 3.1 all-to-all-done
  262.1 2.9 convolution_bitcast_fusion.1.spec_ref
  265.1 8.0 %shard_map.37 = f32[4,512,768]{2,1,0:T(8,128)} custom-call(s32[4]{0:T(128)S(1)} %get-tuple-element.284, f32[2,768,512]{2,1,0:T(8,128)S(1)} %convolution_bitcast_fusion.1.spec_ref, f32[4,512,768]{2,1,0:T(8,128)} %get-tuple-element.137.acc_ref), custom_call_target="tpu_custom_call", output_to_operand_aliasing={{}: (2, {})} | custom-call | tf_op jit(solution)/shard_map/pallas_call | solution.py:114
  273.1 10.0 %convolution_bitcast_fusion.3 = f32[4,256,512]{2,1,0:T(8,128)} fusion(f32[4,512,768]{2,1,0:T(8,128)} %shard_map.37, s32[256]{0:T(256)S(1)} %copy-done.6, s32[768]{0:T(1024)S(1)} %copy-done.2, s32[768]{0:T(1024)S(1)} %copy-done.3, f32[768]{0:T(1024)S(1)} %copy-done.1, pred[768]{0:T(1024)(128)(4,1)S(1)} %copy-done.4, pred[768]{0:T(1024)(128)(4,1)S(1)} %copy-done.5), kind=kOutput, calls=%fused_computation.13 | convolution fusion | flops 2420244480 | bytes 8400384 | tf_op jit(solution)/shard_map/kcr,rl->klc/dot_general | solution.py:168
  283.1 8.1 %all-to-all-start.2 = ((f32[4,256,512]{2,1,0:T(8,128)}), f32[4,256,512]{2,1,0:T(8,128)}, u32[]{:S(2)}, u32[]{:S(2)}) async-start(f32[4,256,512]{2,1,0:T(8,128)} %convolution_bitcast_fusion.3), calls=%async_computation.2 | async-start | bytes 4194304 | tf_op jit(solution)/shard_map/all_to_all | solution.py:169
  291.1 8.0 %shard_map.38 = f32[4,512,768]{2,1,0:T(8,128)} custom-call(s32[4]{0:T(128)S(1)} %get-tuple-element.283, f32[2,768,512]{2,1,0:T(8,128)S(1)} %convolution_bitcast_fusion.1.spec_ref, f32[4,512,768]{2,1,0:T(8,128)} %get-tuple-element.138.acc_ref), custom_call_target="tpu_custom_call", output_to_operand_aliasing={{}: (2, {})} | custom-call | tf_op jit(solution)/shard_map/pallas_call | solution.py:114
  299.1 9.9 %convolution_bitcast_fusion.2 = f32[4,256,512]{2,1,0:T(8,128)} fusion(f32[4,512,768]{2,1,0:T(8,128)} %shard_map.38, s32[256]{0:T(256)S(1)} %copy-done.6, s32[768]{0:T(1024)S(1)} %copy-done.2, s32[768]{0:T(1024)S(1)} %copy-done.3, f32[768]{0:T(1024)S(1)} %copy-done.1, pred[768]{0:T(1024)(128)(4,1)S(1)} %copy-done.4, pred[768]{0:T(1024)(128)(4,1)S(1)} %copy-done.5), kind=kOutput, calls=%fused_computation.12 | convolution fusion | flops 2420244480 | bytes 8400384 | tf_op jit(solution)/shard_map/kcr,rl->klc/dot_general | solution.py:168
  309.1 8.4 %all-to-all-done.2 = f32[4,256,512]{2,1,0:T(8,128)} async-done(((f32[4,256,512]{2,1,0:T(8,128)}), f32[4,256,512]{2,1,0:T(8,128)}, u32[]{:S(2)}, u32[]{:S(2)}) %all-to-all-start.2) | async-done | bytes 2097184 | tf_op jit(solution)/shard_map/all_to_all | solution.py:169
  317.5 4.5 %all-to-all-start.3 = ((f32[4,256,512]{2,1,0:T(8,128)}), f32[4,256,512]{2,1,0:T(8,128)S(1)}, u32[]{:S(2)}, u32[]{:S(2)}) async-start(f32[4,256,512]{2,1,0:T(8,128)} %convolution_bitcast_fusion.2), calls=%async_computation.3 | async-start | bytes 4194304 | tf_op jit(solution)/shard_map/all_to_all | solution.py:169
  323.9 24.3 %all-to-all-done.3 = f32[4,256,512]{2,1,0:T(8,128)S(1)} async-done(((f32[4,256,512]{2,1,0:T(8,128)}), f32[4,256,512]{2,1,0:T(8,128)S(1)}, u32[]{:S(2)}, u32[]{:S(2)}) %all-to-all-start.3) | async-done | bytes 2097184 | tf_op jit(solution)/shard_map/all_to_all | solution.py:169
  (89 shorter events, 50.8 us)
Async XLA Ops:
  0.0 1.2 slice-start
  1.8 0.7 copy-start.8
  4.9 12.5 %copy-start.7 = (f32[64]{0:T(128)S(1)}, f32[64]{0:T(128)}, u32[]{:S(2)}) copy-start(f32[64]{0:T(128)} %param.6) | copy-start | bytes 772
  4.9 34.3 %all-to-all-start.1 = ((f32[32,2,8,768]{3,2,1,0:T(8,128)}), f32[32,2,8,768]{3,2,1,0:T(8,128)S(1)}, u32[]{:S(2)}, u32[]{:S(2)}) async-start(f32[32,2,8,768]{3,2,1,0:T(8,128)} %copy.19), calls=%async_computation.1 | async-start | bytes 3145728 | tf_op jit(solution)/shard_map/all_to_all | solution.py:152
  50.0 25.8 %all-to-all-start = ((f32[32,2,8,768]{3,2,1,0:T(8,128)}), f32[32,2,8,768]{3,2,1,0:T(8,128)S(1)}, u32[]{:S(2)}, u32[]{:S(2)}) async-start(f32[32,2,8,768]{3,2,1,0:T(8,128)} %copy.31), calls=%async_computation | async-start | bytes 3145728 | tf_op jit(solution)/shard_map/while/body/eval_jaxpr/all_to_all | solution.py:152
  80.5 26.2 %all-to-all-start = ((f32[32,2,8,768]{3,2,1,0:T(8,128)}), f32[32,2,8,768]{3,2,1,0:T(8,128)S(1)}, u32[]{:S(2)}, u32[]{:S(2)}) async-start(f32[32,2,8,768]{3,2,1,0:T(8,128)} %copy.31), calls=%async_computation | async-start | bytes 3145728 | tf_op jit(solution)/shard_map/while/body/eval_jaxpr/all_to_all | solution.py:152
  111.2 25.5 %all-to-all-start = ((f32[32,2,8,768]{3,2,1,0:T(8,128)}), f32[32,2,8,768]{3,2,1,0:T(8,128)S(1)}, u32[]{:S(2)}, u32[]{:S(2)}) async-start(f32[32,2,8,768]{3,2,1,0:T(8,128)} %copy.31), calls=%async_computation | async-start | bytes 3145728 | tf_op jit(solution)/shard_map/while/body/eval_jaxpr/all_to_all | solution.py:152
  141.4 26.3 %all-to-all-start = ((f32[32,2,8,768]{3,2,1,0:T(8,128)}), f32[32,2,8,768]{3,2,1,0:T(8,128)S(1)}, u32[]{:S(2)}, u32[]{:S(2)}) async-start(f32[32,2,8,768]{3,2,1,0:T(8,128)} %copy.31), calls=%async_computation | async-start | bytes 3145728 | tf_op jit(solution)/shard_map/while/body/eval_jaxpr/all_to_all | solution.py:152
  172.3 26.2 %all-to-all-start = ((f32[32,2,8,768]{3,2,1,0:T(8,128)}), f32[32,2,8,768]{3,2,1,0:T(8,128)S(1)}, u32[]{:S(2)}, u32[]{:S(2)}) async-start(f32[32,2,8,768]{3,2,1,0:T(8,128)} %copy.31), calls=%async_computation | async-start | bytes 3145728 | tf_op jit(solution)/shard_map/while/body/eval_jaxpr/all_to_all | solution.py:152
  203.1 26.3 %all-to-all-start = ((f32[32,2,8,768]{3,2,1,0:T(8,128)}), f32[32,2,8,768]{3,2,1,0:T(8,128)S(1)}, u32[]{:S(2)}, u32[]{:S(2)}) async-start(f32[32,2,8,768]{3,2,1,0:T(8,128)} %copy.31), calls=%async_computation | async-start | bytes 3145728 | tf_op jit(solution)/shard_map/while/body/eval_jaxpr/all_to_all | solution.py:152
  234.0 26.5 %all-to-all-start = ((f32[32,2,8,768]{3,2,1,0:T(8,128)}), f32[32,2,8,768]{3,2,1,0:T(8,128)S(1)}, u32[]{:S(2)}, u32[]{:S(2)}) async-start(f32[32,2,8,768]{3,2,1,0:T(8,128)} %copy.31), calls=%async_computation | async-start | bytes 3145728 | tf_op jit(solution)/shard_map/while/body/eval_jaxpr/all_to_all | solution.py:152
  260.9 1.2 copy-start
  265.0 8.1 %copy-start.1 = (f32[768]{0:T(1024)S(1)}, f32[768]{0:T(1024)}, u32[]{:S(2)}) copy-start(f32[768]{0:T(1024)} %fusion.34) | copy-start | bytes 9220
  265.0 8.1 %copy-start.2 = (s32[768]{0:T(1024)S(1)}, s32[768]{0:T(1024)}, u32[]{:S(2)}) copy-start(s32[768]{0:T(1024)} %get-tuple-element.179) | copy-start | bytes 9220
  265.0 8.1 %copy-start.3 = (s32[768]{0:T(1024)S(1)}, s32[768]{0:T(1024)}, u32[]{:S(2)}) copy-start(s32[768]{0:T(1024)} %get-tuple-element.180) | copy-start | bytes 9220
  265.0 8.1 %copy-start.4 = (pred[768]{0:T(1024)(128)(4,1)S(1)}, pred[768]{0:T(1024)(128)(4,1)}, u32[]{:S(2)}) copy-start(pred[768]{0:T(1024)(128)(4,1)} %get-tuple-element.181) | copy-start | bytes 2308
  265.0 8.1 %copy-start.5 = (pred[768]{0:T(1024)(128)(4,1)S(1)}, pred[768]{0:T(1024)(128)(4,1)}, u32[]{:S(2)}) copy-start(pred[768]{0:T(1024)(128)(4,1)} %get-tuple-element.182) | copy-start | bytes 2308
  265.1 8.1 %copy-start.6 = (s32[256]{0:T(256)S(1)}, s32[256]{0:T(256)}, u32[]{:S(2)}) copy-start(s32[256]{0:T(256)} %iota_add_fusion.3) | copy-start | bytes 3076
  283.1 34.4 %all-to-all-start.2 = ((f32[4,256,512]{2,1,0:T(8,128)}), f32[4,256,512]{2,1,0:T(8,128)}, u32[]{:S(2)}, u32[]{:S(2)}) async-start(f32[4,256,512]{2,1,0:T(8,128)} %convolution_bitcast_fusion.3), calls=%async_computation.2 | async-start | bytes 4194304 | tf_op jit(solution)/shard_map/all_to_all | solution.py:169
  317.5 30.8 %all-to-all-start.3 = ((f32[4,256,512]{2,1,0:T(8,128)}), f32[4,256,512]{2,1,0:T(8,128)S(1)}, u32[]{:S(2)}, u32[]{:S(2)}) async-start(f32[4,256,512]{2,1,0:T(8,128)} %convolution_bitcast_fusion.2), calls=%async_computation.3 | async-start | bytes 4194304 | tf_op jit(solution)/shard_map/all_to_all | solution.py:169
